TPU v7x, 32 devices: a whole 2x2x4 slice. The times are simulated.
32 devices in a mesh: groups: 2 (over x), wide: 16 (over z, y, core).
Axes of the slice: x: 2, y: 2, z: 4, core: 2. Of those that a mesh axis runs over, the one named last changes fastest.
Arguments:
- activity: bfloat16 [1024, 16, 512], P(('groups', 'wide')), parts along dimension 0, may hold values from -6 to 6
- grad_out: bfloat16 [1024, 16, 512], P('groups', 'wide'), parts along dimension 0, may hold values from -6 to 6
- spatial_weights: bfloat16 [512, 2048], replicated, may hold values from -8 to 8
- temporal_weights: bfloat16 [512, 2048], replicated, may hold values from -8 to 8
- spatial_gain: float32 [512], replicated, may hold values from 0.25 to 1.75
- temporal_gain: float32 [512], replicated, may hold values from 0.25 to 1.75
- adjacency: int32 [16, 16], replicated, may hold values from 0 to 1
- channel_count: int32 [8], P('groups'), parts along dimension 0, may hold values from 128 to 2048
- session_id: int32 [1024], P('groups'), parts along dimension 0, may hold values from 0 to 3, never falling along the last dimension, each value on 1 to 256 neighbouring positions
Outputs:
- layer_out: bfloat16 [1024, 16, 512], P('groups', 'wide'), parts along dimension 0
- grad_activity: bfloat16 [1024, 16, 512], P(('groups', 'wide')), parts along dimension 0
- spatial_grad: float32 [1024, 2048], P(('groups', 'wide')), parts along dimension 0
- temporal_grad: float32 [1024, 2048], P(('groups', 'wide')), parts along dimension 0
There are 2 independent parts, one for each index of `groups`. A program takes and returns all parts, laid end to end along the dimension named above; an argument that names none is the same for every part. Nothing has to cross between parts.
Inputs may be any that keep to these rules, and one draw needn't show every extreme that they name: `session_id`: session ids never fall along time; every session holds 1 to 256 bins, one exactly 256.
All inputs are finite; a program needn't handle non-finite values.
Results may differ from a plain program's by a relative error of at most 0.015.
Values may be sent and summed in bfloat16 or wider, within the bound.
No kernel may reach another device: no remote copies, remote signals or barrier semaphores. Data moves between devices by JAX's collectives and lax.ppermute only.
A program may use at most 192 MiB of HBM per device.

v0:
```python
import jax
import jax.numpy as jnp
from jax import lax
from jax.sharding import PartitionSpec as P

HEADS = 8
eps_norm = 1e-05
block_channels = 128


def norm_inverse(rows):
    values = rows.astype(jnp.float32)
    return lax.rsqrt(jnp.mean(values * values, axis=-1, keepdims=True) + eps_norm)


def norm_forward(rows, gain):
    inverse = norm_inverse(rows)
    return ((rows.astype(jnp.float32) * inverse * gain).astype(jnp.bfloat16), inverse)


def norm_backward(rows, gain, inverse, grad_normed):
    values = rows.astype(jnp.float32)
    scaled = grad_normed * gain
    inner = jnp.mean(values * scaled, axis=-1, keepdims=True)
    return inverse * scaled - values * inverse * inverse * inverse * inner


def normalized_affinity(asking_vectors, lookup_array, admissible_pairs, sharpness_divisor):
    unnormalized_affinities = (
        jnp.einsum(
            "...uo,...ao->...ua", asking_vectors, lookup_array, preferred_element_type=jnp.float32
        )
        * sharpness_divisor
    )
    unnormalized_affinities = jnp.where(admissible_pairs, unnormalized_affinities, -1e30)
    row_max = jnp.max(unnormalized_affinities, axis=-1, keepdims=True)
    expo = jnp.exp(unnormalized_affinities - row_max)
    return expo / jnp.sum(expo, axis=-1, keepdims=True)


def compute_affinity_outputs(
    asking_vectors, lookup_array, payload_array, admissible_pairs, sharpness_divisor
):
    truncated_outcome = normalized_affinity(
        asking_vectors, lookup_array, admissible_pairs, sharpness_divisor
    ).astype(jnp.bfloat16)
    return jnp.einsum(
        "...qk,...kd->...qd", truncated_outcome, payload_array, preferred_element_type=jnp.float32
    ).astype(jnp.bfloat16)


def compute_affinity_derivatives(
    asking_vectors,
    lookup_array,
    payload_array,
    admissible_pairs,
    sharpness_divisor,
    combined_output,
    blended_output_derivative,
):
    coefficient_array = normalized_affinity(
        asking_vectors, lookup_array, admissible_pairs, sharpness_divisor
    )
    truncated_outcome = coefficient_array.astype(jnp.bfloat16)
    grad_values = jnp.einsum(
        "...qk,...qd->...kd",
        truncated_outcome,
        blended_output_derivative,
        preferred_element_type=jnp.float32,
    )
    coefficient_derivative = jnp.einsum(
        "...uo,...ao->...ua",
        blended_output_derivative,
        payload_array,
        preferred_element_type=jnp.float32,
    )
    paired_inner_sums = jnp.sum(
        blended_output_derivative.astype(jnp.float32) * combined_output.astype(jnp.float32),
        axis=-1,
        keepdims=True,
    )
    affinity_derivative = (
        coefficient_array * (coefficient_derivative - paired_inner_sums) * sharpness_divisor
    ).astype(jnp.bfloat16)
    grad_queries = jnp.einsum(
        "...qk,...kd->...qd", affinity_derivative, lookup_array, preferred_element_type=jnp.float32
    )
    grad_keys = jnp.einsum(
        "...qk,...qd->...kd",
        affinity_derivative,
        asking_vectors,
        preferred_element_type=jnp.float32,
    )
    return (
        grad_queries.astype(jnp.bfloat16),
        grad_keys.astype(jnp.bfloat16),
        grad_values.astype(jnp.bfloat16),
    )


def temporal_split(projected):
    pieces = projected.reshape(projected.shape[0], 3, HEADS, projected.shape[1] // (3 * HEADS))
    return [pieces[:, index].transpose(1, 0, 2) for index in range(3)]


def temporal_forward(projected, admissible_pairs):
    asking_vectors, lookup_array, payload_array = temporal_split(projected)
    sharpness_divisor = float(asking_vectors.shape[-1]) ** (-0.5)
    combined_output = compute_affinity_outputs(
        asking_vectors, lookup_array, payload_array, admissible_pairs[None], sharpness_divisor
    )
    return combined_output.transpose(1, 0, 2).reshape(projected.shape[0], -1)


def temporal_backward(projected, admissible_pairs, combined_output, blended_output_derivative):
    asking_vectors, lookup_array, payload_array = temporal_split(projected)
    sharpness_divisor = float(asking_vectors.shape[-1]) ** (-0.5)
    bins = projected.shape[0]
    subspace_outputs = combined_output.reshape(bins, HEADS, -1).transpose(1, 0, 2)
    subspace_derivative = blended_output_derivative.reshape(bins, HEADS, -1).transpose(1, 0, 2)
    derivative_collection = compute_affinity_derivatives(
        asking_vectors,
        lookup_array,
        payload_array,
        admissible_pairs[None],
        sharpness_divisor,
        subspace_outputs,
        subspace_derivative,
    )
    return jnp.stack(derivative_collection, axis=0).transpose(2, 0, 1, 3).reshape(bins, -1)


def spatial_split(projected):
    pieces = projected.reshape(
        projected.shape[0], projected.shape[1], 3, HEADS, projected.shape[2] // (3 * HEADS)
    )
    return [pieces[:, :, index].transpose(0, 2, 1, 3) for index in range(3)]


def spatial_forward(projected, admissible_pairs):
    asking_vectors, lookup_array, payload_array = spatial_split(projected)
    sharpness_divisor = float(asking_vectors.shape[-1]) ** (-0.5)
    combined_output = compute_affinity_outputs(
        asking_vectors, lookup_array, payload_array, admissible_pairs, sharpness_divisor
    )
    return combined_output.transpose(0, 2, 1, 3).reshape(projected.shape[0], projected.shape[1], -1)


def spatial_backward(projected, admissible_pairs, combined_output, blended_output_derivative):
    asking_vectors, lookup_array, payload_array = spatial_split(projected)
    sharpness_divisor = float(asking_vectors.shape[-1]) ** (-0.5)
    bins, blocks = (projected.shape[0], projected.shape[1])
    subspace_outputs = combined_output.reshape(bins, blocks, HEADS, -1).transpose(0, 2, 1, 3)
    subspace_derivative = blended_output_derivative.reshape(bins, blocks, HEADS, -1).transpose(
        0, 2, 1, 3
    )
    derivative_collection = compute_affinity_derivatives(
        asking_vectors,
        lookup_array,
        payload_array,
        admissible_pairs,
        sharpness_divisor,
        subspace_outputs,
        subspace_derivative,
    )
    return (
        jnp.stack(derivative_collection, axis=0).transpose(1, 3, 0, 2, 4).reshape(bins, blocks, -1)
    )


def spatial_allowed(sessions_here, channel_count, adjacency):
    block_count = adjacency.shape[0]
    block_ids = jnp.arange(block_count, dtype=jnp.int32)
    session_pick = (
        sessions_here[:, None] == jnp.arange(channel_count.shape[0], dtype=jnp.int32)[None, :]
    ).astype(jnp.int32)
    count_rows = jnp.sum(session_pick * channel_count[None, :], axis=1)
    live_block = block_ids[None, :] * block_channels < count_rows[:, None]
    linked = adjacency > 0
    itself = block_ids[:, None] == block_ids[None, :]
    admissible_pairs = linked[None, :, :] & live_block[:, None, :] | itself[None, :, :]
    return admissible_pairs[:, None, :, :]


def project(rows, coefficient_array):
    return jnp.einsum("tbd,de->tbe", rows, coefficient_array, preferred_element_type=jnp.float32)


def project_back(derivative_collection, coefficient_array):
    return jnp.einsum(
        "tbe,de->tbd", derivative_collection, coefficient_array, preferred_element_type=jnp.float32
    )


def weight_term(left, right):
    return jnp.einsum("tbd,tbe->de", left, right, preferred_element_type=jnp.float32)


def per_device(
    activity,
    grad_out,
    spatial_weights,
    temporal_weights,
    spatial_gain,
    temporal_gain,
    adjacency,
    channel_count,
    session_id,
):
    local_bins = activity.shape[0]
    model_width = activity.shape[2]
    first_bin = lax.axis_index("wide") * local_bins
    sessions_here = lax.dynamic_slice_in_dim(session_id, first_bin, local_bins)
    normed_one, inverse_one = norm_forward(activity, spatial_gain)
    spatial_proj = project(normed_one, spatial_weights[:, : 3 * model_width]).astype(jnp.bfloat16)
    allowed_space = spatial_allowed(sessions_here, channel_count, adjacency)
    spatial_context = spatial_forward(spatial_proj, allowed_space)
    middle = (
        activity.astype(jnp.float32)
        + project(spatial_context, spatial_weights[:, 3 * model_width :])
    ).astype(jnp.bfloat16)
    middle_block = lax.all_to_all(middle, "wide", split_axis=1, concat_axis=0, tiled=True)
    normed_two, inverse_two = norm_forward(middle_block, temporal_gain)
    temporal_proj = project(normed_two, temporal_weights[:, : 3 * model_width]).astype(jnp.bfloat16)
    allowed_time = session_id[:, None] == session_id[None, :]
    by_block = jnp.moveaxis(temporal_proj, 1, 0)
    temporal_context = jnp.moveaxis(
        lax.map(lambda block_rows: temporal_forward(block_rows, allowed_time), by_block), 0, 1
    )
    layer_out = (
        middle_block.astype(jnp.float32)
        + project(temporal_context, temporal_weights[:, 3 * model_width :])
    ).astype(jnp.bfloat16)
    grad_temporal_context = project_back(grad_out, temporal_weights[:, 3 * model_width :]).astype(
        jnp.bfloat16
    )
    stacked = (
        by_block,
        jnp.moveaxis(temporal_context, 1, 0),
        jnp.moveaxis(grad_temporal_context, 1, 0),
    )
    grad_temporal_proj = jnp.moveaxis(
        lax.map(
            lambda items: temporal_backward(items[0], allowed_time, items[1], items[2]), stacked
        ),
        0,
        1,
    )
    grad_normed_two = project_back(grad_temporal_proj, temporal_weights[:, : 3 * model_width])
    grad_middle = (
        grad_out.astype(jnp.float32)
        + norm_backward(middle_block, temporal_gain, inverse_two, grad_normed_two)
    ).astype(jnp.bfloat16)
    grad_middle_time = lax.all_to_all(grad_middle, "wide", split_axis=0, concat_axis=1, tiled=True)
    normed_cols = normed_two
    context_cols = temporal_context
    temporal_grad = lax.psum_scatter(
        jnp.concatenate(
            [weight_term(normed_cols, grad_temporal_proj), weight_term(context_cols, grad_out)],
            axis=1,
        ).astype(jnp.bfloat16),
        "wide",
        scatter_dimension=0,
        tiled=True,
    ).astype(jnp.float32)
    grad_spatial_context = project_back(
        grad_middle_time, spatial_weights[:, 3 * model_width :]
    ).astype(jnp.bfloat16)
    grad_spatial_proj = spatial_backward(
        spatial_proj, allowed_space, spatial_context, grad_spatial_context
    )
    grad_normed_one = project_back(grad_spatial_proj, spatial_weights[:, : 3 * model_width])
    grad_activity = (
        grad_middle_time.astype(jnp.float32)
        + norm_backward(activity, spatial_gain, inverse_one, grad_normed_one)
    ).astype(jnp.bfloat16)
    normed_cols = normed_one
    context_cols = spatial_context
    spatial_grad = lax.psum_scatter(
        jnp.concatenate(
            [
                weight_term(normed_cols, grad_spatial_proj),
                weight_term(context_cols, grad_middle_time),
            ],
            axis=1,
        ).astype(jnp.bfloat16),
        "wide",
        scatter_dimension=0,
        tiled=True,
    ).astype(jnp.float32)
    return (layer_out, grad_activity, spatial_grad, temporal_grad)


def solution(mesh):
    placed = (
        P(("groups", "wide"), None, None),
        P("groups", "wide", None),
        P(),
        P(),
        P(),
        P(),
        P(),
        P("groups"),
        P("groups"),
    )
    return jax.shard_map(
        per_device,
        mesh=mesh,
        in_specs=placed,
        out_specs=(
            P("groups", "wide", None),
            P(("groups", "wide"), None, None),
            P(("groups", "wide"), None),
            P(("groups", "wide"), None),
        ),
        check_vma=False,
    )
```

profile of v0, /device:TPU:0, one launch (start us, length us, event | category | flops | bytes accessed | tf_op | source)
XLA Modules:
  0.0 230.5 jit_solution(11808287719107655246)
XLA Ops:
  8.4 3.8 %convolution_convert_fusion.2 = bf16[32,16,1536]{2,1,0:T(8,128)(2,1)} fusion(bf16[512,2048]{1,0:T(8,128)(2,1)} %param.11, bf16[32,16,512]{2,1,0:T(8,128)(2,1)} %param.9, f32[512]{0:T(512)} %param.13, f32[32,16]{1,0:T(8,128)S(1)} %add_rsqrt_fusion), kind=kOutput, calls=%fused_computation.15 | convolution fusion | flops 807141376 | bytes 3674112 | tf_op jit(solution)/shard_map/tbd,de->tbe/dot_general | solution.py:186
  12.2 4.0 %reshape.297 = bf16[32,16,3,8,64]{4,3,2,1,0:T(8,128)(2,1)S(1)} reshape(bf16[32,16,1536]{2,1,0:T(8,128)(2,1)} %convolution_convert_fusion.2) | data formatting | bytes 3145728 | tf_op jit(solution)/shard_map/reshape | solution.py:134
  16.2 2.1 fusion.82
  18.9 4.3 %fusion.83 = (f32[32,8,16]{2,1,0:T(8,128)S(1)}, f32[32,8,16,16]{2,3,1,0:T(8,128)}) fusion(pred[32,16,16]{1,2,0:T(8,128)(4,1)S(1)} %and_or_fusion, bf16[32,16,1,8,64]{4,3,2,1,0:T(8,128)(2,1)} %get-tuple-element.29, bf16[32,16,1,8,64]{4,3,2,1,0:T(8,128)(2,1)} %get-tuple-element.28), kind=kOutput, calls=%fused_computation.131 | convolution fusion | flops 8650767 | bytes 1335296 | tf_op jit(solution)/shard_map/sub | solution.py:37
  23.1 2.2 convolution_convert_fusion.6
  30.0 7.4 %all-to-all-start = ((bf16[32,16,512]{2,0,1:T(8,128)(2,1)}), bf16[32,16,512]{2,0,1:T(8,128)(2,1)S(1)}, u32[]{:S(2)}, u32[]{:S(2)}) async-start(bf16[32,16,512]{2,0,1:T(8,128)(2,1)} %copy.98), calls=%async_computation | async-start | bytes 1048576 | tf_op jit(solution)/shard_map/all_to_all | solution.py:222
  38.6 2.3 %convolution_convert_fusion.13 = bf16[512,512]{0,1:T(8,128)(2,1)} fusion(bf16[512,1,512]{2,0,1:T(8,128)(2,1)S(1)} %copy-done.11, bf16[512,2048]{1,0:T(8,128)(2,1)} %param.12), kind=kOutput, calls=%fused_computation.54 | convolution fusion | flops 268697600 | bytes 1572864 | tf_op jit(solution)/shard_map/tbe,de->tbd/dot_general | solution.py:190
  40.9 10.9 %all-to-all-done = bf16[32,16,512]{2,0,1:T(8,128)(2,1)S(1)} async-done(((bf16[32,16,512]{2,0,1:T(8,128)(2,1)}), bf16[32,16,512]{2,0,1:T(8,128)(2,1)S(1)}, u32[]{:S(2)}, u32[]{:S(2)}) %all-to-all-start) | async-done | bytes 524320 | tf_op jit(solution)/shard_map/all_to_all | solution.py:222
  53.3 3.7 %convolution_convert_fusion.1 = bf16[512,1536]{1,0:T(8,128)(2,1)} fusion(bf16[512,2048]{1,0:T(8,128)(2,1)} %param.12, f32[512,512]{0,1:T(8,128)S(1)} %copy.101, f32[512]{0:T(512)S(1)} %copy-done.26, f32[512]{0:T(512)S(1)} %rsqrt.21), kind=kOutput, calls=%fused_computation.14 | convolution fusion | flops 806879232 | bytes 4198400 | tf_op jit(solution)/shard_map/tbd,de->tbe/dot_general | solution.py:186
  58.7 5.4 %fusion.84 = (f32[8,512]{1,0:T(8,128)S(1)}, f32[8,512,512]{1,2,0:T(8,128)}) fusion(pred[512,512]{0,1:T(8,128)(4,1)S(1)} %broadcast_compare_fusion, bf16[512,3,8,64]{0,3,2,1:T(8,128)(2,1)S(1)} %bitcast.171), kind=kOutput, calls=%fused_computation.132 | convolution fusion | flops 276824576 | bytes 9715712 | tf_op jit(solution)/shard_map/while/body/eval_jaxpr/sub | solution.py:37
  64.1 4.7 %fusion.6 = bf16[8,512,512]{1,2,0:T(8,128)(2,1)S(1)} fusion(f32[8,512,512]{1,2,0:T(8,128)} %get-tuple-element.40, f32[8,512]{1,0:T(8,128)S(1)} %get-tuple-element.33), kind=kLoop, calls=%fused_computation.10 | loop fusion | flops 4194304 | bytes 12599296 | tf_op jit(solution)/shard_map/while/body/eval_jaxpr/convert_element_type | solution.py:46
  72.3 1.8 multiply_convert_fusion
  81.5 2.1 reduce.6
  85.0 4.1 %all-to-all-start.1 = ((bf16[16,2,8192]{2,1,0:T(2,128)(2,1)}), bf16[16,2,8192]{2,1,0:T(2,128)(2,1)S(1)}, u32[]{:S(2)}, u32[]{:S(2)}) async-start(bf16[16,2,8192]{2,1,0:T(2,128)(2,1)} %reshape.314), calls=%async_computation.1 | async-start | bytes 1048576 | tf_op jit(solution)/shard_map/all_to_all | solution.py:254
  89.9 2.6 %convolution_convert_fusion = bf16[512,1536]{1,0:T(8,128)(2,1)S(1)} fusion(bf16[512,1536]{0,1:T(8,128)(2,1)} %bitcast.182, f32[512,1,1,1,1,1,512]{6,0,5,4,3,2,1:T(8,128)S(1)} %bitcast.169, f32[512]{0:T(512)S(1)} %copy-done.26, f32[512]{0:T(512)S(1)} %rsqrt.21), kind=kOutput, calls=%fused_computation.13 | convolution fusion | flops 806879232 | bytes 4198400 | tf_op jit(solution)/shard_map/tbd,tbe->de/dot_general | solution.py:196
  94.1 9.4 %all-to-all-done.1 = bf16[16,2,8192]{2,1,0:T(2,128)(2,1)S(1)} async-done(((bf16[16,2,8192]{2,1,0:T(2,128)(2,1)}), bf16[16,2,8192]{2,1,0:T(2,128)(2,1)S(1)}, u32[]{:S(2)}, u32[]{:S(2)}) %all-to-all-start.1) | async-done | bytes 524320 | tf_op jit(solution)/shard_map/all_to_all | solution.py:254
  105.0 2.6 %convolution_convert_fusion.10 = bf16[32,16,512]{2,1,0:T(8,128)(2,1)} fusion(bf16[512,2048]{1,0:T(8,128)(2,1)} %param.11, bf16[16,32,1,512]{3,1,0,2:T(8,128)(2,1)} %bitcast.56), kind=kOutput, calls=%fused_computation.51 | convolution fusion | flops 268697600 | bytes 1572864 | tf_op jit(solution)/shard_map/tbe,de->tbd/dot_general | solution.py:190
  116.5 3.0 %reshape.305 = bf16[32,16,1536]{2,1,0:T(8,128)(2,1)} reshape(bf16[32,16,3,8,64]{4,3,2,1,0:T(8,128)(2,1)S(1)} %copy.115) | data formatting | bytes 3145728 | tf_op jit(solution)/shard_map/reshape | solution.py:167
  119.5 1.9 fusion.28
  125.5 2.4 %fusion.31 = bf16[512,1,512]{2,0,1:T(8,128)(2,1)} fusion(f32[512,512]{1,0:T(8,128)S(1)} %bitcast.170, bf16[512,512]{0,1:T(8,128)(2,1)S(1)} %bitcast.177, bf16[512,2048]{1,0:T(8,128)(2,1)} %param.12), kind=kOutput, calls=%fused_computation.60 | convolution fusion | flops 268959744 | bytes 2621440 | tf_op jit(solution)/shard_map/tbd,de->tbe/dot_general | solution.py:186
  127.9 2.5 %fusion.42 = (f32[32,16]{1,0:T(8,128)S(1)}, f32[32,16,512]{2,1,0:T(8,128)S(1)}) fusion(bf16[32,16,512]{2,1,0:T(8,128)(2,1)S(1)} %copy-done.14, f32[512]{0:T(512)S(1)} %copy-done.27, bf16[32,16,1536]{2,1,0:T(8,128)(2,1)S(1)} %copy-done.19, bf16[512,2048]{1,0:T(8,128)(2,1)} %param.11), kind=kOutput, calls=%fused_computation.71 | convolution fusion | flops 806354432 | bytes 4722688 | tf_op jit(solution)/shard_map/tbe,de->tbd/dot_general | solution.py:190
  130.4 2.3 %fusion.40 = bf16[32,16,512]{2,1,0:T(8,128)(2,1)} fusion(bf16[32,16,512]{2,1,0:T(8,128)(2,1)S(1)} %copy-done.14, f32[32,16,512]{2,1,0:T(8,128)S(1)} %get-tuple-element.46, f32[32,16]{1,0:T(8,128)S(1)} %broadcast_multiply_fusion, f32[32,16]{1,0:T(8,128)S(1)} %add_rsqrt_fusion, bf16[16,32,1,512]{3,1,0,2:T(8,128)(2,1)} %bitcast.56), kind=kLoop, calls=%fused_computation.69 | loop fusion | flops 2621440 | bytes 2625536 | tf_op jit(solution)/shard_map/convert_element_type | solution.py:276
  132.8 24.4 %reduce-scatter.5.cloned.1.call-done = bf16[32,2048]{1,0:T(8,128)(2,1)} async-done(((bf16[512,2048]{1,0:T(8,128)(2,1)}), bf16[32,2048]{1,0:T(8,128)(2,1)}) %reduce-scatter.5.cloned.1.call-update) | async-done | bytes 131088 | tf_op jit(solution)/shard_map/reduce_scatter | solution.py:257
  158.8 63.2 %reduce-scatter.3.cloned.1.call-done = bf16[32,2048]{1,0:T(8,128)(2,1)} async-done(((bf16[512,2048]{1,0:T(8,128)(2,1)}), bf16[32,2048]{1,0:T(8,128)(2,1)}) %reduce-scatter.3.cloned.1.call-update) | async-done | bytes 131088 | tf_op jit(solution)/shard_map/reduce_scatter | solution.py:279
  (116 shorter events, 42.8 us)
Async XLA Ops:
  16.2 2.2 copy-start.25
  16.2 2.2 copy-start.24
  16.2 2.3 %copy-start.28 = (s32[4]{0:T(128)S(1)}, s32[4]{0:T(128)}, u32[]{:S(2)}) copy-start(s32[4]{0:T(128)} %param.16) | copy-start | bytes 52
  18.8 4.3 %copy-start.20 = (bf16[32,16,1,8,64]{4,3,2,1,0:T(8,128)(2,1)S(1)}, bf16[32,16,1,8,64]{4,3,2,1,0:T(8,128)(2,1)}, u32[]{:S(2)}) copy-start(bf16[32,16,1,8,64]{4,3,2,1,0:T(8,128)(2,1)} %get-tuple-element.30) | copy-start | bytes 1572868
  27.2 2.8 %copy-start.22 = (bf16[32,16,512]{2,1,0:T(8,128)(2,1)}, bf16[32,16,512]{2,1,0:T(8,128)(2,1)S(1)}, u32[]{:S(2)}) copy-start(bf16[32,16,512]{2,1,0:T(8,128)(2,1)S(1)} %reshape.298) | copy-start | bytes 1572868
  27.2 10.2 %copy-start.11 = (bf16[512,1,512]{2,0,1:T(8,128)(2,1)S(1)}, bf16[512,1,512]{2,0,1:T(8,128)(2,1)}, u32[]{:S(2)}) copy-start(bf16[512,1,512]{2,0,1:T(8,128)(2,1)} %param.10) | copy-start | bytes 1572868
  30.0 21.9 %all-to-all-start = ((bf16[32,16,512]{2,0,1:T(8,128)(2,1)}), bf16[32,16,512]{2,0,1:T(8,128)(2,1)S(1)}, u32[]{:S(2)}, u32[]{:S(2)}) async-start(bf16[32,16,512]{2,0,1:T(8,128)(2,1)} %copy.98), calls=%async_computation | async-start | bytes 1048576 | tf_op jit(solution)/shard_map/all_to_all | solution.py:222
  40.9 12.4 %copy-start.26 = (f32[512]{0:T(512)S(1)}, f32[512]{0:T(512)}, u32[]{:S(2)}) copy-start(f32[512]{0:T(512)} %param.14) | copy-start | bytes 6148
  52.0 37.9 %copy-start = (f32[32,16,512]{2,0,1:T(8,128)}, f32[32,16,512]{2,0,1:T(8,128)S(1)}, u32[]{:S(2)}) copy-start(f32[32,16,512]{2,0,1:T(8,128)S(1)} %convert_element_type.236) | copy-start | bytes 3145732
  64.1 4.7 %copy-start.16 = (bf16[512,512]{0,1:T(8,128)(2,1)S(1)}, bf16[512,512]{0,1:T(8,128)(2,1)}, u32[]{:S(2)}) copy-start(bf16[512,512]{0,1:T(8,128)(2,1)} %convolution_convert_fusion.13) | copy-start | bytes 1572868
  68.8 3.6 %copy-start.2 = (f32[8,512,512]{1,2,0:T(8,128)S(1)}, f32[8,512,512]{1,2,0:T(8,128)}, u32[]{:S(2)}) copy-start(f32[8,512,512]{1,2,0:T(8,128)} %get-tuple-element.40) | copy-start | bytes 25165828
  69.6 19.8 %copy-start.3 = (bf16[8,512,64]{1,2,0:T(8,128)(2,1)}, bf16[8,512,64]{1,2,0:T(8,128)(2,1)S(1)}, u32[]{:S(2)}) copy-start(bf16[8,512,64]{1,2,0:T(8,128)(2,1)S(1)} %get-tuple-element.42) | copy-start | bytes 1572868
  76.3 2.5 %copy-start.23 = (bf16[512,2048]{1,0:T(8,128)(2,1)S(1)}, bf16[512,2048]{1,0:T(8,128)(2,1)}, u32[]{:S(2)}) copy-start(bf16[512,2048]{1,0:T(8,128)(2,1)} %param.12) | copy-start | bytes 6291460
  76.5 3.3 %copy-start.17 = (bf16[3,8,512,64]{2,3,1,0:T(8,128)(2,1)}, bf16[3,8,512,64]{2,3,1,0:T(8,128)(2,1)S(1)}, u32[]{:S(2)}) copy-start(bf16[3,8,512,64]{2,3,1,0:T(8,128)(2,1)S(1)} %pad_maximum_fusion.2) | copy-start | bytes 4718596
  81.5 7.9 %copy-start.12 = (bf16[512,1,512]{2,0,1:T(8,128)(2,1)S(1)}, bf16[512,1,512]{2,0,1:T(8,128)(2,1)}, u32[]{:S(2)}) copy-start(bf16[512,1,512]{2,0,1:T(8,128)(2,1)} %param.10) | copy-start | bytes 1572868
  85.0 18.6 %all-to-all-start.1 = ((bf16[16,2,8192]{2,1,0:T(2,128)(2,1)}), bf16[16,2,8192]{2,1,0:T(2,128)(2,1)S(1)}, u32[]{:S(2)}, u32[]{:S(2)}) async-start(bf16[16,2,8192]{2,1,0:T(2,128)(2,1)} %reshape.314), calls=%async_computation.1 | async-start | bytes 1048576 | tf_op jit(solution)/shard_map/all_to_all | solution.py:254
  89.1 68.1 %reduce-scatter.5.cloned.1.call-start = ((), (), s32[]{:S(2)}) async-start(), calls=%async_computation.5 | async-start | bytes 2228224 | tf_op jit(solution)/shard_map/reduce_scatter | solution.py:257
  94.1 127.9 %reduce-scatter.3.cloned.1.call-start = ((), (), s32[]{:S(2)}) async-start(), calls=%async_computation.4 | async-start | bytes 2228224 | tf_op jit(solution)/shard_map/reduce_scatter | solution.py:279
  105.0 4.3 %copy-start.8 = (bf16[32,8,16,64]{3,2,1,0:T(8,128)(2,1)S(1)}, bf16[32,8,16,64]{3,2,1,0:T(8,128)(2,1)}, u32[]{:S(2)}) copy-start(bf16[32,8,16,64]{3,2,1,0:T(8,128)(2,1)} %copy-done.7) | copy-start | bytes 1572868
  107.6 2.4 %copy-start.21 = (bf16[32,16,1,8,64]{4,3,2,1,0:T(8,128)(2,1)S(1)}, bf16[32,16,1,8,64]{4,3,2,1,0:T(8,128)(2,1)}, u32[]{:S(2)}) copy-start(bf16[32,16,1,8,64]{4,3,2,1,0:T(8,128)(2,1)} %get-tuple-element.30) | copy-start | bytes 1572868
  119.5 1.9 copy-start.14
  119.5 2.0 copy-start.18
  119.5 2.0 copy-start.27
  125.5 2.4 %copy-start.19 = (bf16[32,16,1536]{2,1,0:T(8,128)(2,1)S(1)}, bf16[32,16,1536]{2,1,0:T(8,128)(2,1)}, u32[]{:S(2)}) copy-start(bf16[32,16,1536]{2,1,0:T(8,128)(2,1)} %reshape.305) | copy-start | bytes 4718596
  (10 other events, 13.1 us)
Sparse Core Ops, SparseCore 0:
  94.2 62.9 reduce-scatter.4
  161.4 60.6 reduce-scatter.2
where the time goes:
time: 232 us; the launch traced here: 230 us
  waiting for transfers between devices  108 us (47%)
  matrix products  46.6 us (20%)
  local copies, waits for them, and re-layouts  29.2 us (13%)
  other arithmetic  20.3 us (9%)
  between operations  14.6 us (6%)
  starting transfers between devices  11.8 us (5%)
    reduce_scatter x1, waiting for transfers between devices, per_device(): lax.psum_scatter(jnp.concatenate([weight_term(normed_cols, grad_spatial_p...  63.2 us
    reduce_scatter x1, waiting for transfers between devices, per_device(): lax.psum_scatter(jnp.concatenate([weight_term(normed_cols, grad_temporal_...  24.4 us
    unnamed x66, local copies, waits for them, and re-layouts  12.8 us
    dot_general x4, matrix products, project(): jnp.einsum('tbd,de->tbe', rows, coefficient_array, preferred_element_type...  11.6 us
    all_to_all x1, waiting for transfers between devices, per_device(): lax.all_to_all(middle, 'wide', split_axis=1, concat_axis=0, tiled=True)  10.9 us
    sub x2, matrix products, normalized_affinity(): expo = jnp.exp(unnormalized_affinities - row_max)  9.67 us
    all_to_all x1, waiting for transfers between devices, per_device(): lax.all_to_all(grad_middle, 'wide', split_axis=0, concat_axis=1, tiled=True)  9.45 us
    dot_general x4, matrix products, project_back(): jnp.einsum('tbe,de->tbd', derivative_collection, coefficient_array, prefe...  8.39 us
  transfers between devices with their start and end apart: 4, of which 4 were waited for; matrix products, arithmetic and copies ran while one was open for 15% of the time, Pallas kernels for 0%

commit v1 on v0

--- a/solution.py
+++ b/solution.py
@@ -6,6 +6,18 @@
 HEADS = 8
 eps_norm = 1e-05
 block_channels = 128
+
+
+def in_blocks(x, dim, peers):
+    shape = x.shape
+    pieces = x.reshape(*shape[:dim], peers, shape[dim] // peers, *shape[dim + 1 :])
+    return jnp.moveaxis(pieces, dim, 0)
+
+
+def joined_along(tiles, dim):
+    tiles = jnp.moveaxis(tiles, 0, dim)
+    shape = tiles.shape
+    return tiles.reshape(*shape[:dim], shape[dim] * shape[dim + 1], *shape[dim + 2 :])
 
 
 def norm_inverse(rows):
@@ -219,7 +231,14 @@
         activity.astype(jnp.float32)
         + project(spatial_context, spatial_weights[:, 3 * model_width :])
     ).astype(jnp.bfloat16)
-    middle_block = lax.all_to_all(middle, "wide", split_axis=1, concat_axis=0, tiled=True)
+    devices, here = (lax.axis_size("wide"), lax.axis_index("wide"))
+    blocks_2 = in_blocks(middle, 1, devices)
+    done = [blocks_2[here]]
+    for hop in range(1, devices):
+        sent = blocks_2[here ^ hop]
+        done.append(lax.ppermute(sent, "wide", [(i, i ^ hop) for i in range(devices)]))
+    blocks_2 = jnp.stack(done)[here ^ jnp.arange(devices)]
+    middle_block = joined_along(blocks_2, 0)
     normed_two, inverse_two = norm_forward(middle_block, temporal_gain)
     temporal_proj = project(normed_two, temporal_weights[:, : 3 * model_width]).astype(jnp.bfloat16)
     allowed_time = session_id[:, None] == session_id[None, :]

time: 232 us -> 270 us (1.16)
  waiting for transfers between devices: 108 us -> 143 us
  starting transfers between devices: 11.8 us -> 20.3 us
  matrix products: 46.6 us -> 42 us
    ppermute x0 -> x15, waiting for transfers between devices: none -> 44.7 us  [per_device(): lax.ppermute(sent, 'wide', [(i, i ^ hop) for i in range(devices)])]
    ppermute x0 -> x15, starting transfers between devices: none -> 16.6 us  [per_device(): lax.ppermute(sent, 'wide', [(i, i ^ hop) for i in range(devices)])]
    all_to_all x1 -> x0, waiting for transfers between devices: 10.9 us -> none  [per_device(): lax.all_to_all(middle, 'wide', split_axis=1, concat_axis=0, tiled=True)]
    all_to_all x1 -> x0, starting transfers between devices: 7.39 us -> none  [per_device(): lax.all_to_all(middle, 'wide', split_axis=1, concat_axis=0, tiled=True)]
    unnamed x66 -> x80, local copies, waits for them, and re-layouts: 12.8 us -> 13.3 us
  transfers between devices with their start and end apart: 4 -> 18, of which waited for: 4 -> 13; matrix products, arithmetic and copies ran while one was open for 15% -> 11% of each run, Pallas kernels for 0% -> 0%
where the time goes in v1:
time: 270 us; the launch traced here: 269 us
  waiting for transfers between devices  143 us (53%)
  matrix products  42 us (16%)
  local copies, waits for them, and re-layouts  30.4 us (11%)
  starting transfers between devices  20.3 us (8%)
  other arithmetic  18.3 us (7%)
  between operations  14.9 us (6%)
    reduce_scatter x1, waiting for transfers between devices, per_device(): lax.psum_scatter(jnp.concatenate([weight_term(normed_cols, grad_spatial_p...  63.2 us
    ppermute x15, waiting for transfers between devices, per_device(): lax.ppermute(sent, 'wide', [(i, i ^ hop) for i in range(devices)])  44.7 us
    reduce_scatter x1, waiting for transfers between devices, per_device(): lax.psum_scatter(jnp.concatenate([weight_term(normed_cols, grad_temporal_...  25.3 us
    ppermute x15, starting transfers between devices, per_device(): lax.ppermute(sent, 'wide', [(i, i ^ hop) for i in range(devices)])  16.6 us
    unnamed x80, local copies, waits for them, and re-layouts  13.3 us
    dot_general x4, matrix products, project(): jnp.einsum('tbd,de->tbe', rows, coefficient_array, preferred_element_type...  11.4 us
    all_to_all x1, waiting for transfers between devices, per_device(): lax.all_to_all(grad_middle, 'wide', split_axis=0, concat_axis=1, tiled=True)  9.75 us
    sub x2, matrix products, normalized_affinity(): expo = jnp.exp(unnormalized_affinities - row_max)  8.35 us
  transfers between devices with their start and end apart: 18, of which 13 were waited for; matrix products, arithmetic and copies ran while one was open for 11% of the time, Pallas kernels for 0%

profile of v1, /device:TPU:0, one launch (start us, length us, event | category | flops | bytes accessed | tf_op | source)
XLA Modules:
  0.0 268.8 jit_solution(14773185842125897377)
XLA Ops:
  9.3 3.8 %convolution_convert_fusion.2 = bf16[32,16,1536]{2,1,0:T(8,128)(2,1)} fusion(bf16[512,2048]{1,0:T(8,128)(2,1)} %param.11, bf16[32,16,512]{2,1,0:T(8,128)(2,1)} %param.9, f32[512]{0:T(512)} %param.13, f32[32,16]{1,0:T(8,128)S(1)} %add_rsqrt_fusion), kind=kOutput, calls=%fused_computation.16 | convolution fusion | flops 807141376 | bytes 3674112 | tf_op jit(solution)/shard_map/tbd,de->tbe/dot_general | solution.py:198
  13.1 4.0 %reshape.381 = bf16[32,16,3,8,64]{4,3,2,1,0:T(8,128)(2,1)S(1)} reshape(bf16[32,16,1536]{2,1,0:T(8,128)(2,1)} %convolution_convert_fusion.2) | data formatting | bytes 3145728 | tf_op jit(solution)/shard_map/reshape | solution.py:146
  19.6 2.9 %fusion.83 = (f32[32,8,16]{2,1,0:T(8,128)S(1)}, f32[32,8,16,16]{2,3,1,0:T(8,128)S(1)}) fusion(pred[32,16,16]{1,2,0:T(8,128)(4,1)S(1)} %and_or_fusion, bf16[32,16,1,8,64]{4,3,2,1,0:T(8,128)(2,1)} %get-tuple-element.29, bf16[32,16,1,8,64]{4,3,2,1,0:T(8,128)(2,1)} %get-tuple-element.28), kind=kOutput, calls=%fused_computation.167 | convolution fusion | flops 8650767 | bytes 1335296 | tf_op jit(solution)/shard_map/sub | solution.py:49
  29.7 5.5 %collective-permute-start.14 = (bf16[32,1,512]{2,1,0:T(2,128)(2,1)S(1)}, bf16[32,1,512]{2,1,0:T(2,128)(2,1)S(1)}, u32[]{:S(2)}, u32[]{:S(2)}) collective-permute-start(bf16[32,1,512]{2,1,0:T(2,128)(2,1)S(1)} %get-tuple-element.31), channel_id=1, source_target_pairs={{0,15},{1,14},{2,13},{3,12},{4,11},{5,10},{6,9},{7,8},{8,7},{9,6},... | collective-permute-start | bytes 98312 | tf_op jit(solution)/shard_map/ppermute | solution.py:239
  35.8 3.1 %collective-permute-start.12 = (bf16[32,1,512]{2,1,0:T(2,128)(2,1)S(1)}, bf16[32,1,512]{2,1,0:T(2,128)(2,1)S(1)}, u32[]{:S(2)}, u32[]{:S(2)}) collective-permute-start(bf16[32,1,512]{2,1,0:T(2,128)(2,1)S(1)} %get-tuple-element.33), channel_id=1, source_target_pairs={{0,13},{1,12},{2,15},{3,14},{4,9},{5,8},{6,11},{7,10},{8,5},{9,4},... | collective-permute-start | bytes 98312 | tf_op jit(solution)/shard_map/ppermute | solution.py:239
  43.4 3.1 %collective-permute-done.1 = bf16[32,1,512]{2,1,0:T(2,128)(2,1)S(1)} collective-permute-done((bf16[32,1,512]{2,1,0:T(2,128)(2,1)S(1)}, bf16[32,1,512]{2,1,0:T(2,128)(2,1)S(1)}, u32[]{:S(2)}, u32[]{:S(2)}) %collective-permute-start.1) | collective-permute-done | bytes 32800 | tf_op jit(solution)/shard_map/ppermute | solution.py:239
  47.2 3.6 %collective-permute-done.2 = bf16[32,1,512]{2,1,0:T(2,128)(2,1)S(1)} collective-permute-done((bf16[32,1,512]{2,1,0:T(2,128)(2,1)S(1)}, bf16[32,1,512]{2,1,0:T(2,128)(2,1)S(1)}, u32[]{:S(2)}, u32[]{:S(2)}) %collective-permute-start.2) | collective-permute-done | bytes 32800 | tf_op jit(solution)/shard_map/ppermute | solution.py:239
  50.9 4.3 %collective-permute-done.3 = bf16[32,1,512]{2,1,0:T(2,128)(2,1)S(1)} collective-permute-done((bf16[32,1,512]{2,1,0:T(2,128)(2,1)S(1)}, bf16[32,1,512]{2,1,0:T(2,128)(2,1)S(1)}, u32[]{:S(2)}, u32[]{:S(2)}) %collective-permute-start.3) | collective-permute-done | bytes 32800 | tf_op jit(solution)/shard_map/ppermute | solution.py:239
  55.1 3.7 %collective-permute-done.4 = bf16[32,1,512]{2,1,0:T(2,128)(2,1)S(1)} collective-permute-done((bf16[32,1,512]{2,1,0:T(2,128)(2,1)S(1)}, bf16[32,1,512]{2,1,0:T(2,128)(2,1)S(1)}, u32[]{:S(2)}, u32[]{:S(2)}) %collective-permute-start.4) | collective-permute-done | bytes 32800 | tf_op jit(solution)/shard_map/ppermute | solution.py:239
  59.9 4.1 %collective-permute-done.5 = bf16[32,1,512]{2,1,0:T(2,128)(2,1)S(1)} collective-permute-done((bf16[32,1,512]{2,1,0:T(2,128)(2,1)S(1)}, bf16[32,1,512]{2,1,0:T(2,128)(2,1)S(1)}, u32[]{:S(2)}, u32[]{:S(2)}) %collective-permute-start.5) | collective-permute-done | bytes 32800 | tf_op jit(solution)/shard_map/ppermute | solution.py:239
  64.2 4.4 %collective-permute-done.6 = bf16[32,1,512]{2,1,0:T(2,128)(2,1)S(1)} collective-permute-done((bf16[32,1,512]{2,1,0:T(2,128)(2,1)S(1)}, bf16[32,1,512]{2,1,0:T(2,128)(2,1)S(1)}, u32[]{:S(2)}, u32[]{:S(2)}) %collective-permute-start.6) | collective-permute-done | bytes 32800 | tf_op jit(solution)/shard_map/ppermute | solution.py:239
  68.6 3.0 %collective-permute-start.7 = (bf16[32,1,512]{2,1,0:T(2,128)(2,1)S(1)}, bf16[32,1,512]{2,1,0:T(2,128)(2,1)S(1)}, u32[]{:S(2)}, u32[]{:S(2)}) collective-permute-start(bf16[32,1,512]{2,1,0:T(2,128)(2,1)S(1)} %get-tuple-element.44), channel_id=1, source_target_pairs={{0,8},{1,9},{2,10},{3,11},{4,12},{5,13},{6,14},{7,15},{8,0},{9,1},... | collective-permute-start | bytes 98312 | tf_op jit(solution)/shard_map/ppermute | solution.py:239
  71.6 3.8 %collective-permute-done.7 = bf16[32,1,512]{2,1,0:T(2,128)(2,1)S(1)} collective-permute-done((bf16[32,1,512]{2,1,0:T(2,128)(2,1)S(1)}, bf16[32,1,512]{2,1,0:T(2,128)(2,1)S(1)}, u32[]{:S(2)}, u32[]{:S(2)}) %collective-permute-start.7) | collective-permute-done | bytes 32800 | tf_op jit(solution)/shard_map/ppermute | solution.py:239
  75.4 6.2 %collective-permute-done.8 = bf16[32,1,512]{2,1,0:T(2,128)(2,1)S(1)} collective-permute-done((bf16[32,1,512]{2,1,0:T(2,128)(2,1)S(1)}, bf16[32,1,512]{2,1,0:T(2,128)(2,1)S(1)}, u32[]{:S(2)}, u32[]{:S(2)}) %collective-permute-start.8) | collective-permute-done | bytes 32800 | tf_op jit(solution)/shard_map/ppermute | solution.py:239
  82.0 5.6 %collective-permute-done.9 = bf16[32,1,512]{2,1,0:T(2,128)(2,1)S(1)} collective-permute-done((bf16[32,1,512]{2,1,0:T(2,128)(2,1)S(1)}, bf16[32,1,512]{2,1,0:T(2,128)(2,1)S(1)}, u32[]{:S(2)}, u32[]{:S(2)}) %collective-permute-start.9) | collective-permute-done | bytes 32800 | tf_op jit(solution)/shard_map/ppermute | solution.py:239
  87.6 6.0 %collective-permute-done.10 = bf16[32,1,512]{2,1,0:T(2,128)(2,1)S(1)} collective-permute-done((bf16[32,1,512]{2,1,0:T(2,128)(2,1)S(1)}, bf16[32,1,512]{2,1,0:T(2,128)(2,1)S(1)}, u32[]{:S(2)}, u32[]{:S(2)}) %collective-permute-start.10) | collective-permute-done | bytes 32800 | tf_op jit(solution)/shard_map/ppermute | solution.py:239
  94.8 3.6 %convolution_convert_fusion.1 = bf16[512,1536]{1,0:T(8,128)(2,1)} fusion(bf16[512,512]{1,0:T(8,128)(2,1)S(1)} %multiply_convert_fusion.3, bf16[512,2048]{1,0:T(8,128)(2,1)} %param.12), kind=kOutput, calls=%fused_computation.15 | convolution fusion | flops 806092800 | bytes 3670016 | tf_op jit(solution)/shard_map/tbd,de->tbe/dot_general | solution.py:198
  100.1 5.4 %fusion.84 = (f32[8,512]{1,0:T(8,128)S(1)}, f32[8,512,512]{1,2,0:T(8,128)}) fusion(pred[512,512]{0,1:T(8,128)(4,1)S(1)} %broadcast_compare_fusion, bf16[512,3,8,64]{0,3,2,1:T(8,128)(2,1)S(1)} %bitcast.205), kind=kOutput, calls=%fused_computation.168 | convolution fusion | flops 276824576 | bytes 9715712 | tf_op jit(solution)/shard_map/while/body/eval_jaxpr/sub | solution.py:49
  105.5 4.7 %fusion.6 = bf16[8,512,512]{1,2,0:T(8,128)(2,1)S(1)} fusion(f32[8,512,512]{1,2,0:T(8,128)} %get-tuple-element.56, f32[8,512]{1,0:T(8,128)S(1)} %get-tuple-element.55), kind=kLoop, calls=%fused_computation.11 | loop fusion | flops 4194304 | bytes 12599296 | tf_op jit(solution)/shard_map/while/body/eval_jaxpr/convert_element_type | solution.py:58
  124.2 3.6 %all-to-all-start = ((bf16[16,2,8192]{2,1,0:T(2,128)(2,1)}), bf16[16,2,8192]{2,1,0:T(2,128)(2,1)S(1)}, u32[]{:S(2)}, u32[]{:S(2)}) async-start(bf16[16,2,8192]{2,1,0:T(2,128)(2,1)} %reshape.412), calls=%async_computation | async-start | bytes 1048576 | tf_op jit(solution)/shard_map/all_to_all | solution.py:273
  132.5 9.8 %all-to-all-done = bf16[16,2,8192]{2,1,0:T(2,128)(2,1)S(1)} async-done(((bf16[16,2,8192]{2,1,0:T(2,128)(2,1)}), bf16[16,2,8192]{2,1,0:T(2,128)(2,1)S(1)}, u32[]{:S(2)}, u32[]{:S(2)}) %all-to-all-start) | async-done | bytes 524320 | tf_op jit(solution)/shard_map/all_to_all | solution.py:273
  155.0 3.0 %reshape.389 = bf16[32,16,1536]{2,1,0:T(8,128)(2,1)} reshape(bf16[32,16,3,8,64]{4,3,2,1,0:T(8,128)(2,1)S(1)} %copy.483) | data formatting | bytes 3145728 | tf_op jit(solution)/shard_map/reshape | solution.py:179
  170.2 25.3 %reduce-scatter.5.cloned.1.call-done = bf16[32,2048]{1,0:T(8,128)(2,1)} async-done(((bf16[512,2048]{1,0:T(8,128)(2,1)}), bf16[32,2048]{1,0:T(8,128)(2,1)}) %reduce-scatter.5.cloned.1.call-update) | async-done | bytes 131088 | tf_op jit(solution)/shard_map/reduce_scatter | solution.py:276
  197.1 63.2 %reduce-scatter.3.cloned.1.call-done = bf16[32,2048]{1,0:T(8,128)(2,1)} async-done(((bf16[512,2048]{1,0:T(8,128)(2,1)}), bf16[32,2048]{1,0:T(8,128)(2,1)}) %reduce-scatter.3.cloned.1.call-update) | async-done | bytes 131088 | tf_op jit(solution)/shard_map/reduce_scatter | solution.py:298
  (161 shorter events, 68.4 us)
Async XLA Ops:
  19.6 4.3 %copy-start.19 = (bf16[32,16,1,8,64]{4,3,2,1,0:T(8,128)(2,1)S(1)}, bf16[32,16,1,8,64]{4,3,2,1,0:T(8,128)(2,1)}, u32[]{:S(2)}) copy-start(bf16[32,16,1,8,64]{4,3,2,1,0:T(8,128)(2,1)} %get-tuple-element.30) | copy-start | bytes 1572868
  26.4 13.4 %copy-start.9 = (bf16[512,1,512]{2,0,1:T(8,128)(2,1)S(1)}, bf16[512,1,512]{2,0,1:T(8,128)(2,1)}, u32[]{:S(2)}) copy-start(bf16[512,1,512]{2,0,1:T(8,128)(2,1)} %param.10) | copy-start | bytes 1572868
  29.7 64.0 %collective-permute-start.14 = (bf16[32,1,512]{2,1,0:T(2,128)(2,1)S(1)}, bf16[32,1,512]{2,1,0:T(2,128)(2,1)S(1)}, u32[]{:S(2)}, u32[]{:S(2)}) collective-permute-start(bf16[32,1,512]{2,1,0:T(2,128)(2,1)S(1)} %get-tuple-element.31), channel_id=1, source_target_pairs={{0,15},{1,14},{2,13},{3,12},{4,11},{5,10},{6,9},{7,8},{8,7},{9,6},... | collective-permute-start | bytes 98312 | tf_op jit(solution)/shard_map/ppermute | solution.py:239
  35.2 58.5 %collective-permute-start.13 = (bf16[32,1,512]{2,1,0:T(2,128)(2,1)S(1)}, bf16[32,1,512]{2,1,0:T(2,128)(2,1)S(1)}, u32[]{:S(2)}, u32[]{:S(2)}) collective-permute-start(bf16[32,1,512]{2,1,0:T(2,128)(2,1)S(1)} %get-tuple-element.32), channel_id=1, source_target_pairs={{0,14},{1,15},{2,12},{3,13},{4,10},{5,11},{6,8},{7,9},{8,6},{9,7},... | collective-permute-start | bytes 98312 | tf_op jit(solution)/shard_map/ppermute | solution.py:239
  35.8 57.8 %collective-permute-start.12 = (bf16[32,1,512]{2,1,0:T(2,128)(2,1)S(1)}, bf16[32,1,512]{2,1,0:T(2,128)(2,1)S(1)}, u32[]{:S(2)}, u32[]{:S(2)}) collective-permute-start(bf16[32,1,512]{2,1,0:T(2,128)(2,1)S(1)} %get-tuple-element.33), channel_id=1, source_target_pairs={{0,13},{1,12},{2,15},{3,14},{4,9},{5,8},{6,11},{7,10},{8,5},{9,4},... | collective-permute-start | bytes 98312 | tf_op jit(solution)/shard_map/ppermute | solution.py:239
  39.0 54.7 %collective-permute-start.11 = (bf16[32,1,512]{2,1,0:T(2,128)(2,1)S(1)}, bf16[32,1,512]{2,1,0:T(2,128)(2,1)S(1)}, u32[]{:S(2)}, u32[]{:S(2)}) collective-permute-start(bf16[32,1,512]{2,1,0:T(2,128)(2,1)S(1)} %get-tuple-element.40), channel_id=1, source_target_pairs={{0,12},{1,13},{2,14},{3,15},{4,8},{5,9},{6,10},{7,11},{8,4},{9,5},... | collective-permute-start | bytes 98312 | tf_op jit(solution)/shard_map/ppermute | solution.py:239
  39.3 2.8 %collective-permute-start = (bf16[32,1,512]{2,1,0:T(2,128)(2,1)S(1)}, bf16[32,1,512]{2,1,0:T(2,128)(2,1)S(1)}, u32[]{:S(2)}, u32[]{:S(2)}) collective-permute-start(bf16[32,1,512]{2,1,0:T(2,128)(2,1)S(1)} %get-tuple-element.51), channel_id=1, source_target_pairs={{0,1},{1,0},{2,3},{3,2},{4,5},{5,4},{6,7},{7,6},{8,9},{9,8},{10,11... | collective-permute-start | bytes 98312 | tf_op jit(solution)/shard_map/ppermute | solution.py:239
  39.8 54.9 %copy-start.24 = (f32[512]{0:T(512)S(1)}, f32[512]{0:T(512)}, u32[]{:S(2)}) copy-start(f32[512]{0:T(512)} %param.14) | copy-start | bytes 6148
  42.1 4.4 %collective-permute-start.1 = (bf16[32,1,512]{2,1,0:T(2,128)(2,1)S(1)}, bf16[32,1,512]{2,1,0:T(2,128)(2,1)S(1)}, u32[]{:S(2)}, u32[]{:S(2)}) collective-permute-start(bf16[32,1,512]{2,1,0:T(2,128)(2,1)S(1)} %get-tuple-element.50), channel_id=1, source_target_pairs={{0,2},{1,3},{2,0},{3,1},{4,6},{5,7},{6,4},{7,5},{8,10},{9,11},{10,... | collective-permute-start | bytes 98312 | tf_op jit(solution)/shard_map/ppermute | solution.py:239
  46.5 4.4 %collective-permute-start.2 = (bf16[32,1,512]{2,1,0:T(2,128)(2,1)S(1)}, bf16[32,1,512]{2,1,0:T(2,128)(2,1)S(1)}, u32[]{:S(2)}, u32[]{:S(2)}) collective-permute-start(bf16[32,1,512]{2,1,0:T(2,128)(2,1)S(1)} %get-tuple-element.49), channel_id=1, source_target_pairs={{0,3},{1,2},{2,1},{3,0},{4,7},{5,6},{6,5},{7,4},{8,11},{9,10},{10,... | collective-permute-start | bytes 98312 | tf_op jit(solution)/shard_map/ppermute | solution.py:239
  50.9 4.3 %collective-permute-start.3 = (bf16[32,1,512]{2,1,0:T(2,128)(2,1)S(1)}, bf16[32,1,512]{2,1,0:T(2,128)(2,1)S(1)}, u32[]{:S(2)}, u32[]{:S(2)}) collective-permute-start(bf16[32,1,512]{2,1,0:T(2,128)(2,1)S(1)} %get-tuple-element.48), channel_id=1, source_target_pairs={{0,4},{1,5},{2,6},{3,7},{4,0},{5,1},{6,2},{7,3},{8,12},{9,13},{10,... | collective-permute-start | bytes 98312 | tf_op jit(solution)/shard_map/ppermute | solution.py:239
  55.1 3.7 %collective-permute-start.4 = (bf16[32,1,512]{2,1,0:T(2,128)(2,1)S(1)}, bf16[32,1,512]{2,1,0:T(2,128)(2,1)S(1)}, u32[]{:S(2)}, u32[]{:S(2)}) collective-permute-start(bf16[32,1,512]{2,1,0:T(2,128)(2,1)S(1)} %get-tuple-element.47), channel_id=1, source_target_pairs={{0,5},{1,4},{2,7},{3,6},{4,1},{5,0},{6,3},{7,2},{8,13},{9,12},{10,... | collective-permute-start | bytes 98312 | tf_op jit(solution)/shard_map/ppermute | solution.py:239
  58.8 5.2 %collective-permute-start.5 = (bf16[32,1,512]{2,1,0:T(2,128)(2,1)S(1)}, bf16[32,1,512]{2,1,0:T(2,128)(2,1)S(1)}, u32[]{:S(2)}, u32[]{:S(2)}) collective-permute-start(bf16[32,1,512]{2,1,0:T(2,128)(2,1)S(1)} %get-tuple-element.46), channel_id=1, source_target_pairs={{0,6},{1,7},{2,4},{3,5},{4,2},{5,3},{6,0},{7,1},{8,14},{9,15},{10,... | collective-permute-start | bytes 98312 | tf_op jit(solution)/shard_map/ppermute | solution.py:239
  64.0 4.6 %collective-permute-start.6 = (bf16[32,1,512]{2,1,0:T(2,128)(2,1)S(1)}, bf16[32,1,512]{2,1,0:T(2,128)(2,1)S(1)}, u32[]{:S(2)}, u32[]{:S(2)}) collective-permute-start(bf16[32,1,512]{2,1,0:T(2,128)(2,1)S(1)} %get-tuple-element.45), channel_id=1, source_target_pairs={{0,7},{1,6},{2,5},{3,4},{4,3},{5,2},{6,1},{7,0},{8,15},{9,14},{10,... | collective-permute-start | bytes 98312 | tf_op jit(solution)/shard_map/ppermute | solution.py:239
  68.6 6.8 %collective-permute-start.7 = (bf16[32,1,512]{2,1,0:T(2,128)(2,1)S(1)}, bf16[32,1,512]{2,1,0:T(2,128)(2,1)S(1)}, u32[]{:S(2)}, u32[]{:S(2)}) collective-permute-start(bf16[32,1,512]{2,1,0:T(2,128)(2,1)S(1)} %get-tuple-element.44), channel_id=1, source_target_pairs={{0,8},{1,9},{2,10},{3,11},{4,12},{5,13},{6,14},{7,15},{8,0},{9,1},... | collective-permute-start | bytes 98312 | tf_op jit(solution)/shard_map/ppermute | solution.py:239
  75.3 6.2 %collective-permute-start.8 = (bf16[32,1,512]{2,1,0:T(2,128)(2,1)S(1)}, bf16[32,1,512]{2,1,0:T(2,128)(2,1)S(1)}, u32[]{:S(2)}, u32[]{:S(2)}) collective-permute-start(bf16[32,1,512]{2,1,0:T(2,128)(2,1)S(1)} %get-tuple-element.43), channel_id=1, source_target_pairs={{0,9},{1,8},{2,11},{3,10},{4,13},{5,12},{6,15},{7,14},{8,1},{9,0},... | collective-permute-start | bytes 98312 | tf_op jit(solution)/shard_map/ppermute | solution.py:239
  81.5 6.1 %collective-permute-start.9 = (bf16[32,1,512]{2,1,0:T(2,128)(2,1)S(1)}, bf16[32,1,512]{2,1,0:T(2,128)(2,1)S(1)}, u32[]{:S(2)}, u32[]{:S(2)}) collective-permute-start(bf16[32,1,512]{2,1,0:T(2,128)(2,1)S(1)} %get-tuple-element.42), channel_id=1, source_target_pairs={{0,10},{1,11},{2,8},{3,9},{4,14},{5,15},{6,12},{7,13},{8,2},{9,3},... | collective-permute-start | bytes 98312 | tf_op jit(solution)/shard_map/ppermute | solution.py:239
  87.6 6.0 %collective-permute-start.10 = (bf16[32,1,512]{2,1,0:T(2,128)(2,1)S(1)}, bf16[32,1,512]{2,1,0:T(2,128)(2,1)S(1)}, u32[]{:S(2)}, u32[]{:S(2)}) collective-permute-start(bf16[32,1,512]{2,1,0:T(2,128)(2,1)S(1)} %get-tuple-element.41), channel_id=1, source_target_pairs={{0,11},{1,10},{2,9},{3,8},{4,15},{5,14},{6,13},{7,12},{8,3},{9,2},... | collective-permute-start | bytes 98312 | tf_op jit(solution)/shard_map/ppermute | solution.py:239
  105.5 4.7 %copy-start.14 = (bf16[512,512]{0,1:T(8,128)(2,1)S(1)}, bf16[512,512]{0,1:T(8,128)(2,1)}, u32[]{:S(2)}) copy-start(bf16[512,512]{0,1:T(8,128)(2,1)} %convolution_convert_fusion.13) | copy-start | bytes 1572868
  111.0 17.0 %copy-start.1 = (bf16[8,512,64]{1,2,0:T(8,128)(2,1)}, bf16[8,512,64]{1,2,0:T(8,128)(2,1)S(1)}, u32[]{:S(2)}) copy-start(bf16[8,512,64]{1,2,0:T(8,128)(2,1)S(1)} %get-tuple-element.58) | copy-start | bytes 1572868
  124.2 18.1 %all-to-all-start = ((bf16[16,2,8192]{2,1,0:T(2,128)(2,1)}), bf16[16,2,8192]{2,1,0:T(2,128)(2,1)S(1)}, u32[]{:S(2)}, u32[]{:S(2)}) async-start(bf16[16,2,8192]{2,1,0:T(2,128)(2,1)} %reshape.412), calls=%async_computation | async-start | bytes 1048576 | tf_op jit(solution)/shard_map/all_to_all | solution.py:273
  127.8 67.7 %reduce-scatter.5.cloned.1.call-start = ((), (), s32[]{:S(2)}) async-start(), calls=%async_computation.4 | async-start | bytes 2228224 | tf_op jit(solution)/shard_map/reduce_scatter | solution.py:276
  132.5 127.8 %reduce-scatter.3.cloned.1.call-start = ((), (), s32[]{:S(2)}) async-start(), calls=%async_computation.3 | async-start | bytes 2228224 | tf_op jit(solution)/shard_map/reduce_scatter | solution.py:298
  142.9 4.9 %copy-start.6 = (bf16[32,8,16,64]{3,2,1,0:T(8,128)(2,1)S(1)}, bf16[32,8,16,64]{3,2,1,0:T(8,128)(2,1)}, u32[]{:S(2)}) copy-start(bf16[32,8,16,64]{3,2,1,0:T(8,128)(2,1)} %copy-done.5) | copy-start | bytes 1572868
  (25 other events, 49.8 us)
Sparse Core Ops, SparseCore 0:
  132.6 62.8 reduce-scatter.4
  199.7 60.5 reduce-scatter.2
